TPU v7x, 512 devices: a whole 4x4x16 slice. The times are simulated.
512 devices in a mesh: graph: 32 (over z, core), irreps: 16 (over y, x).
Axes of the slice: x: 4, y: 4, z: 16, core: 2. Of those that a mesh axis runs over, the one named last changes fastest.
Arguments:
- node_feats: bfloat16 [49, 128, 2048], P(None, 'irreps', 'graph'), may hold values from -8 to 8
- norm_gain: float32 [7, 128], P(None, 'irreps'), may hold values from 0.1 to 1.9
- species: int32 [2048], P('graph'), may hold values from 0 to 89
- send_list: int32 [8192], P('graph'), may hold values from 0 to 63
- edge_source: int32 [32768], P('graph'), may hold values from 0 to 319, as said below
- edge_target: int32 [32768], P('graph'), may hold values from 0 to 63
- edge_count: int32 [32], P('graph'), may hold values from 512 to 1024, as said below
- edge_length: float32 [32768], P('graph'), may hold values from 0.8 to 6
- wigner: bfloat16 [235, 32768], P(None, 'graph'), may hold values from -2.5 to 2.5
- radial_in: bfloat16 [512, 128], replicated, may hold values from -0.25 to 0.25
- species_table: bfloat16 [90, 128], replicated, may hold values from -6 to 6
- radial_out: bfloat16 [128, 896], replicated, may hold values from -0.5 to 0.5
- order_zero: bfloat16 [896, 896], replicated, may hold values from -0.1875 to 0.1875
- order_one: bfloat16 [2, 768, 768], replicated, may hold values from -0.15625 to 0.15625
- order_two: bfloat16 [2, 640, 640], replicated, may hold values from -0.15625 to 0.15625
- project_weight: bfloat16 [7, 128, 128], P(None, None, 'irreps'), may hold values from -0.5 to 0.5
Outputs:
- new_feats: bfloat16 [49, 128, 2048], P(None, 'irreps', 'graph')
Inputs may be any that keep to these rules, and one draw needn't show every extreme that they name: `edge_source`: an index into the table of its edge's domain. A domain reads no slot of its own send block; from each other domain it reads only the first few slots (between 1 and 8 of them), and it reads slot 7 of some domain. `edge_count`: edge slots at or past a domain's count are padding; some domain has all 1024 live.
All inputs are finite; a program needn't handle non-finite values.
Results may differ from a plain program's by a relative error of at most 0.006.
Values may be sent and summed in bfloat16 or wider, within the bound.
No kernel may reach another device: no remote copies, remote signals or barrier semaphores. Data moves between devices by JAX's collectives and lax.ppermute only.
A program may use at most 128 MiB of HBM per device.

v0:
```python
import jax
import jax.numpy as jnp
import numpy as np
from jax import lax
from jax.sharding import PartitionSpec as P

CHANNELS = 128
MAX_DEGREE = 6
MAX_ORDER = 2
ROTATED = 29
EPSILON = 1e-06
CUTOFF = 6.0


def order_index(degree, harmonic):
    if harmonic == 0:
        return degree
    first_row = MAX_DEGREE + 1
    for level in range(1, abs(harmonic)):
        first_row = first_row + 2 * (MAX_DEGREE + 1 - level)
    if harmonic < 0:
        first_row = first_row + MAX_DEGREE + 1 - abs(harmonic)
    return first_row + degree - abs(harmonic)


def wigner_start(degree):
    running = 0
    for level in range(degree):
        running = running + (2 * min(level, MAX_ORDER) + 1) * (2 * level + 1)
    return running


def left_dot(weight, values):
    return lax.dot_general(
        weight, values, (((0,), (0,)), ((), ())), preferred_element_type=jnp.float32
    )


def degree_sums(squares):
    return jnp.stack(
        [
            jnp.sum(squares[degree * degree : (degree + 1) ** 2], axis=0)
            for degree in range(MAX_DEGREE + 1)
        ]
    )


def normalize(node_feats, norm_gain, totals):
    levels = MAX_DEGREE + 1
    degree_of = np.repeat(np.arange(levels), 2 * np.arange(levels) + 1)
    entry_counts = (2 * np.arange(levels) + 1) * CHANNELS
    inverse = 1.0 / jnp.sqrt(totals / jnp.asarray(entry_counts, jnp.float32)[:, None] + EPSILON)
    gain_rows = norm_gain[degree_of]
    scale_rows = inverse[degree_of]
    return (node_feats.astype(jnp.float32) * gain_rows[:, :, None] * scale_rows[:, None, :]).astype(
        jnp.bfloat16
    )


def normalize_rows(values, gain_full, totals):
    levels = MAX_DEGREE + 1
    degree_of = np.repeat(np.arange(levels), 2 * np.arange(levels) + 1)
    entry_counts = (2 * np.arange(levels) + 1) * CHANNELS
    inverse = 1.0 / jnp.sqrt(totals / jnp.asarray(entry_counts, jnp.float32)[:, None] + EPSILON)
    gain_rows = gain_full[degree_of]
    scale_rows = inverse[degree_of]
    return (values * gain_rows[:, :, None] * scale_rows[:, None, :]).astype(jnp.bfloat16)


def rotate(source, wig_rows):
    pieces = [None] * ROTATED
    for degree in range(MAX_DEGREE + 1):
        reach_order = min(degree, MAX_ORDER)
        span_cols = 2 * degree + 1
        first_row = wigner_start(degree)
        for position in range(2 * reach_order + 1):
            total = None
            for column in range(span_cols):
                term = (
                    wig_rows[first_row + position * span_cols + column][None, :]
                    * source[degree * degree + column]
                )
                total = term if total is None else total + term
            pieces[order_index(degree, position - reach_order)] = total
    return jnp.stack(pieces).astype(jnp.bfloat16)


def unrotate(gated, wig_rows):
    pieces = []
    for degree in range(MAX_DEGREE + 1):
        reach_order = min(degree, MAX_ORDER)
        span_cols = 2 * degree + 1
        first_row = wigner_start(degree)
        for column in range(span_cols):
            total = None
            for position in range(2 * reach_order + 1):
                term = (
                    wig_rows[first_row + position * span_cols + column][None, :]
                    * gated[order_index(degree, position - reach_order)]
                )
                total = term if total is None else total + term
            pieces.append(total)
    return jnp.stack(pieces)


def radial_weights(lengths, kind_ids, radial_in, species_table, radial_out):
    basis_count = radial_in.shape[0]
    spacing = CUTOFF / (basis_count - 1)
    centers = jnp.arange(basis_count, dtype=jnp.float32) * spacing
    basis_rows = jnp.exp(
        -0.5 * jnp.square((lengths[None, :] - centers[:, None]) / (2.0 * spacing))
    ).astype(jnp.bfloat16)
    onehot = (
        kind_ids[None, :] == jnp.arange(species_table.shape[0], dtype=jnp.int32)[:, None]
    ).astype(jnp.bfloat16)
    hidden = jax.nn.silu(left_dot(radial_in, basis_rows) + left_dot(species_table, onehot)).astype(
        jnp.bfloat16
    )
    return left_dot(radial_out, hidden)


def convolve(rotated, radial, order_zero, order_one, order_two):
    levels = MAX_DEGREE + 1
    channel_count = rotated.shape[1]
    num_edges = rotated.shape[2]
    lowest = (
        rotated[:levels].astype(jnp.float32).reshape(levels * channel_count, num_edges) * radial
    ).astype(jnp.bfloat16)
    outputs = [left_dot(order_zero, lowest).reshape(levels, channel_count, num_edges)]
    first_row = levels
    for harmonic, weight in ((1, order_one), (2, order_two)):
        span_rows = levels - harmonic
        plus_rows = rotated[first_row : first_row + span_rows].reshape(
            span_rows * channel_count, num_edges
        )
        minus_rows = rotated[first_row + span_rows : first_row + 2 * span_rows].reshape(
            span_rows * channel_count, num_edges
        )
        joined = jnp.concatenate([plus_rows, minus_rows], axis=1)
        real_part = left_dot(weight[0], joined)
        cross_part = left_dot(weight[1], joined)
        outputs.append(
            (real_part[:, :num_edges] - cross_part[:, num_edges:]).reshape(
                span_rows, channel_count, num_edges
            )
        )
        outputs.append(
            (cross_part[:, :num_edges] + real_part[:, num_edges:]).reshape(
                span_rows, channel_count, num_edges
            )
        )
        first_row = first_row + 2 * span_rows
    mixed = jnp.concatenate(outputs, axis=0)
    scalar = mixed[0]
    return jnp.concatenate(
        [jax.nn.silu(scalar)[None], mixed[1:] * jax.nn.sigmoid(scalar)[None]], axis=0
    ).astype(jnp.bfloat16)


def split_dot(values, weight):
    upper_part = values.astype(jnp.bfloat16)
    lower_part = (values - upper_part.astype(jnp.float32)).astype(jnp.bfloat16)
    return jnp.dot(upper_part, weight, preferred_element_type=jnp.float32) + jnp.dot(
        lower_part, weight, preferred_element_type=jnp.float32
    )


def body(
    node_feats,
    norm_gain,
    species,
    send_list,
    edge_source,
    edge_target,
    edge_count,
    edge_length,
    wigner,
    radial_in,
    species_table,
    radial_out,
    order_zero,
    order_one,
    order_two,
    project_weight,
):
    levels = MAX_DEGREE + 1
    owners = lax.axis_size("irreps")
    quarter = lax.axis_index("irreps")
    coeffs, span_chan, atom_count = node_feats.shape
    per_owner = edge_source.shape[0] // owners
    first_edge = quarter * per_owner
    outgoing = node_feats[:, :, send_list]
    arrived = lax.all_to_all(outgoing, "graph", split_axis=2, concat_axis=2, tiled=True)
    packed = jnp.concatenate(
        [norm_gain, project_weight.astype(jnp.float32).reshape(levels, -1)], axis=1
    )
    spread = lax.all_to_all(
        jnp.broadcast_to(packed[None], (owners,) + packed.shape), "irreps", 0, 0, tiled=True
    )
    gain_full = jnp.transpose(spread[:, :, :span_chan], (1, 0, 2)).reshape(
        levels, owners * span_chan
    )
    weight_full = jnp.transpose(
        spread[:, :, span_chan:].reshape(owners, levels, CHANNELS, span_chan), (1, 2, 0, 3)
    ).reshape(levels, CHANNELS, owners * span_chan)
    lookup = jnp.concatenate([node_feats, arrived], axis=2)
    source = lax.all_to_all(
        lookup[:, :, edge_source], "irreps", split_axis=2, concat_axis=1, tiled=True
    )
    source = source.astype(jnp.float32)
    squares = jnp.sum(jnp.square(source), axis=1)
    totals = degree_sums(squares)
    normed = normalize_rows(source, gain_full, totals)
    wig_mine = lax.dynamic_slice_in_dim(wigner, first_edge, per_owner, 1).astype(jnp.float32)
    rotated = rotate(normed.astype(jnp.float32), wig_mine)
    targets_mine = lax.dynamic_slice_in_dim(edge_target, first_edge, per_owner)
    lengths_mine = lax.dynamic_slice_in_dim(edge_length, first_edge, per_owner)
    radial = radial_weights(
        lengths_mine, species[targets_mine], radial_in, species_table, radial_out
    )
    gated = convolve(rotated, radial, order_zero, order_one, order_two)
    messages = unrotate(gated.astype(jnp.float32), wig_mine)
    edge_weight = jnp.where(
        first_edge + jnp.arange(per_owner, dtype=jnp.int32) < edge_count[0], 0.25, 0.0
    ).astype(jnp.float32)
    onehot = jnp.where(
        targets_mine[:, None] == jnp.arange(atom_count, dtype=jnp.int32)[None, :],
        edge_weight[:, None],
        0.0,
    ).astype(jnp.bfloat16)
    summed = split_dot(messages.reshape(-1, per_owner), onehot).reshape(
        coeffs, CHANNELS, atom_count
    )
    upper_part = summed.astype(jnp.bfloat16)
    lower_part = (summed - upper_part.astype(jnp.float32)).astype(jnp.bfloat16)
    updates = []
    for degree in range(levels):
        rows = slice(degree * degree, (degree + 1) ** 2)
        weight = weight_full[degree].astype(jnp.bfloat16)
        updates.append(
            jnp.einsum("io,jia->oja", weight, upper_part[rows], preferred_element_type=jnp.float32)
            + jnp.einsum(
                "io,jia->oja", weight, lower_part[rows], preferred_element_type=jnp.float32
            )
        )
    projected = jnp.concatenate(updates, axis=1)
    returned = lax.all_to_all(
        projected.reshape(owners, span_chan, coeffs, atom_count), "irreps", 0, 0, tiled=True
    )
    total = jnp.transpose(jnp.sum(returned, axis=0), (1, 0, 2))
    return (node_feats.astype(jnp.float32) + total).astype(jnp.bfloat16)


def solution(mesh):
    return jax.shard_map(
        body,
        mesh=mesh,
        in_specs=(
            P(None, "irreps", "graph"),
            P(None, "irreps"),
            P("graph"),
            P("graph"),
            P("graph"),
            P("graph"),
            P("graph"),
            P("graph"),
            P(None, "graph"),
            P(),
            P(),
            P(),
            P(),
            P(),
            P(),
            P(None, None, "irreps"),
        ),
        out_specs=P(None, "irreps", "graph"),
        check_vma=False,
    )
```

profile of v0, /device:TPU:2, one launch (start us, length us, event | category | flops | bytes accessed | tf_op | source)
XLA Modules:
  0.0 238.1 jit_solution(476793149073174638)
XLA Ops:
  3.4 2.0 reshape.3035
  5.5 15.5 %all-to-all-start.1 = ((bf16[32,2,1568]{2,1,0:T(2,128)(2,1)}), bf16[32,2,1568]{2,1,0:T(2,128)(2,1)S(1)}, u32[]{:S(2)}, u32[]{:S(2)}) async-start(bf16[32,2,1568]{2,1,0:T(2,128)(2,1)} %reshape.3035), calls=%async_computation.1 | async-start | bytes 425984 | tf_op jit(solution)/shard_map/all_to_all | solution.py:193
  30.8 1.3 compare_select_fusion.2
  34.0 7.6 %all-to-all-done.1 = bf16[32,2,1568]{2,1,0:T(2,128)(2,1)S(1)} async-done(((bf16[32,2,1568]{2,1,0:T(2,128)(2,1)}), bf16[32,2,1568]{2,1,0:T(2,128)(2,1)S(1)}, u32[]{:S(2)}, u32[]{:S(2)}) %all-to-all-start.1) | async-done | bytes 200736 | tf_op jit(solution)/shard_map/all_to_all | solution.py:193
  42.6 7.5 %all-to-all-start = ((f32[16,7,1032]{2,1,0:T(8,128)}), f32[16,7,1032]{2,1,0:T(8,128)}, u32[]{:S(2)}, u32[]{:S(2)}) async-start(f32[16,7,1032]{2,1,0:T(8,128)} %broadcast_in_dim.56), calls=%async_computation | async-start | bytes 1179648 | tf_op jit(solution)/shard_map/all_to_all | solution.py:197
  50.0 1.6 reshape.3036
  51.8 7.7 %gather_fusion.1 = bf16[1024,49,8]{1,2,0:T(8,128)(2,1)} fusion(bf16[49,8,320]{0,1,2:T(8,128)(2,1)S(1)} %pad_maximum_fusion, s32[1024]{0:T(1024)S(1)} %get-tuple-element.263), kind=kCustom, calls=%fused_computation.1 | custom fusion | bytes 1609728 | tf_op jit(solution)/shard_map/gather | solution.py:208
  59.5 3.1 %bitcast_bitcast_fusion = bf16[1024,8,49]{2,1,0:T(8,128)(2,1)} fusion(bf16[1024,49,8]{1,2,0:T(8,128)(2,1)} %gather_fusion.1), kind=kLoop, calls=%fused_computation.490 | loop fusion | bytes 1605632
  62.6 5.8 %reshape.3037 = bf16[16,2,12544]{2,1,0:T(2,128)(2,1)} reshape(bf16[1024,8,49]{2,1,0:T(8,128)(2,1)} %bitcast_bitcast_fusion) | data formatting | bytes 1605632
  68.4 7.4 %all-to-all-start.2 = ((bf16[16,2,12544]{2,1,0:T(2,128)(2,1)}), bf16[16,2,12544]{2,1,0:T(2,128)(2,1)S(1)}, u32[]{:S(2)}, u32[]{:S(2)}) async-start(bf16[16,2,12544]{2,1,0:T(2,128)(2,1)} %reshape.3037), calls=%async_computation.2 | async-start | bytes 1605632 | tf_op jit(solution)/shard_map/all_to_all | solution.py:207
  78.7 1.6 copy.222
  80.4 2.4 %fusion.73 = (bf16[1,128,16,8]{2,3,1,0:T(8,128)(2,1)S(1)}, bf16[1,128,16,8]{2,3,1,0:T(8,128)(2,1)S(1)}, bf16[1,128,16,8]{2,3,1,0:T(8,128)(2,1)S(1)}, bf16[1,128,...) fusion(bf16[7,128,16,8]{2,3,1,0:T(8,128)(2,1)} %bitcast.748), kind=kLoop, calls=%fused_computation.487 | loop fusion | bytes 458752 | tf_op jit(solution)/shard_map/slice | solution.py:239
  82.8 1.8 copy.223
  85.5 1.8 copy.244
  87.3 1.8 copy.248
  92.8 7.4 %reshape.3038 = bf16[1024,8,49]{2,1,0:T(8,128)(2,1)} reshape(bf16[16,2,12544]{2,1,0:T(2,128)(2,1)S(1)} %all-to-all-done.2) | data formatting | bytes 1605632
  100.2 3.1 %multiply_reduce_fusion = f32[49,1024]{0,1:T(8,128)S(1)} fusion(bf16[1024,8,49]{2,1,0:T(8,128)(2,1)} %reshape.3038), kind=kLoop, calls=%fused_computation.6 | loop fusion | flops 1154048 | bytes 1003520 | tf_op jit(solution)/shard_map/reduce_sum | solution.py:211
  104.4 4.9 %copy.226 = f32[49,8,16,64]{3,1,2,0:T(8,128)} copy(bf16[49,8,16,64]{0,1,3,2:T(8,128)(2,1)} %bitcast.745) | data formatting | bytes 2408448 | tf_op jit(solution)/shard_map/convert_element_type | solution.py:210
  109.4 3.4 %copy.228 = f32[49,128,64]{1,2,0:T(8,128)} copy(f32[49,128,64]{2,1,0:T(8,128)} %bitcast.746) | data formatting | bytes 3211264 | tf_op jit(solution)/shard_map/convert_element_type | solution.py:210
  113.7 1.9 fusion.17
  120.7 1.6 constant_dynamic-update-slice_fusion.29
  122.3 1.4 constant_dynamic-update-slice_fusion.25
  123.7 1.4 constant_dynamic-update-slice_fusion.18
  139.6 1.4 constant_dynamic-update-slice_fusion
  141.0 1.5 fusion.9
  189.9 1.6 bitcast_dynamic-update-slice_fusion.8
  195.8 2.1 copy.322
  198.0 3.0 %reshape.3039 = f32[16,1,25088]{2,1,0:T(1,128)} reshape(f32[16,49,8,64]{3,2,1,0:T(8,128)S(1)} %bitcast.747) | data formatting | bytes 3211264
  200.9 27.3 %all_to_all.24 = f32[16,1,25088]{2,1,0:T(1,128)S(1)} all-to-all(f32[16,1,25088]{2,1,0:T(1,128)} %reshape.3039), channel_id=1, replica_groups=mesh['graph'=32,'irreps'=16] {'irreps'}, dimensions={0} | all-to-all | bytes 3211264 | tf_op jit(solution)/shard_map/all_to_all | solution.py:247
  228.7 4.5 %reduce.4 = f32[16,25088]{1,0:T(8,128)S(1)} reduce(f32[16,1,25088]{2,1,0:T(1,128)S(1)} %all_to_all.24, f32[]{:T(128)} %broadcast.1939), dimensions={1}, to_apply=%all_to_all.19.reduce_sub_computation | reduce | bytes 3211268 | tf_op jit(solution)/shard_map/all_to_all | solution.py:247
  233.2 2.0 reshape.3040
  235.3 2.2 bitcast_reduce_fusion
  (757 shorter events, 92.9 us)
Async XLA Ops:
  0.0 141.0 %copy-start = (bf16[896,896]{1,0:T(8,128)(2,1)S(1)}, bf16[896,896]{1,0:T(8,128)(2,1)}, u32[]{:S(2)}) copy-start(bf16[896,896]{1,0:T(8,128)(2,1)} %param.32) | copy-start | bytes 4816900
  0.0 29.8 %copy-start.16 = (bf16[7,128,8]{1,2,0:T(8,128)(2,1)S(1)}, bf16[7,128,8]{1,2,0:T(8,128)(2,1)}, u32[]{:S(2)}) copy-start(bf16[7,128,8]{1,2,0:T(8,128)(2,1)} %param.35) | copy-start | bytes 43012
  3.4 29.5 %copy-start.274 = (s32[1024]{0:T(1024)S(1)}, s32[1024]{0:T(1024)}, u32[]{:S(2)}) copy-start(s32[1024]{0:T(1024)} %param.24) | copy-start | bytes 12292
  3.4 30.2 %copy-start.275 = (f32[7,8]{1,0:T(8,128)S(1)}, f32[7,8]{1,0:T(8,128)}, u32[]{:S(2)}) copy-start(f32[7,8]{1,0:T(8,128)} %param.21) | copy-start | bytes 676
  3.4 30.3 %copy-start.278 = (bf16[512,128]{1,0:T(8,128)(2,1)S(1)}, bf16[512,128]{1,0:T(8,128)(2,1)}, u32[]{:S(2)}) copy-start(bf16[512,128]{1,0:T(8,128)(2,1)} %param.29) | copy-start | bytes 393220
  5.5 36.2 %all-to-all-start.1 = ((bf16[32,2,1568]{2,1,0:T(2,128)(2,1)}), bf16[32,2,1568]{2,1,0:T(2,128)(2,1)S(1)}, u32[]{:S(2)}, u32[]{:S(2)}) async-start(bf16[32,2,1568]{2,1,0:T(2,128)(2,1)} %reshape.3035), calls=%async_computation.1 | async-start | bytes 425984 | tf_op jit(solution)/shard_map/all_to_all | solution.py:193
  25.2 108.9 %copy-start.23 = (f32[64]{0:T(128)}, f32[64]{0:T(128)S(1)}, u32[]{:S(2)}) copy-start(f32[64]{0:T(128)S(1)} %get-tuple-element.48) | copy-start | bytes 772
  25.2 108.9 %copy-start.25 = (f32[64]{0:T(128)}, f32[64]{0:T(128)S(1)}, u32[]{:S(2)}) copy-start(f32[64]{0:T(128)S(1)} %get-tuple-element.49) | copy-start | bytes 772
  42.6 25.9 %all-to-all-start = ((f32[16,7,1032]{2,1,0:T(8,128)}), f32[16,7,1032]{2,1,0:T(8,128)}, u32[]{:S(2)}, u32[]{:S(2)}) async-start(f32[16,7,1032]{2,1,0:T(8,128)} %broadcast_in_dim.56), calls=%async_computation | async-start | bytes 1179648 | tf_op jit(solution)/shard_map/all_to_all | solution.py:197
  62.6 13.8 %copy-start.2 = (s32[64]{0:T(128)S(1)}, s32[64]{0:T(128)}, u32[]{:S(2)}) copy-start(s32[64]{0:T(128)} %param.22) | copy-start | bytes 772
  68.4 24.4 %all-to-all-start.2 = ((bf16[16,2,12544]{2,1,0:T(2,128)(2,1)}), bf16[16,2,12544]{2,1,0:T(2,128)(2,1)S(1)}, u32[]{:S(2)}, u32[]{:S(2)}) async-start(bf16[16,2,12544]{2,1,0:T(2,128)(2,1)} %reshape.3037), calls=%async_computation.2 | async-start | bytes 1605632 | tf_op jit(solution)/shard_map/all_to_all | solution.py:207
  147.0 13.1 %copy-start.88 = (f32[64]{0:T(128)S(1)}, f32[64]{0:T(128)}, u32[]{:S(2)}) copy-start(f32[64]{0:T(128)} %get-tuple-element.56) | copy-start | bytes 772
  147.8 13.1 %copy-start.78 = (f32[64]{0:T(128)S(1)}, f32[64]{0:T(128)}, u32[]{:S(2)}) copy-start(f32[64]{0:T(128)} %get-tuple-element.55) | copy-start | bytes 772
  148.6 13.1 %copy-start.66 = (f32[64]{0:T(128)S(1)}, f32[64]{0:T(128)}, u32[]{:S(2)}) copy-start(f32[64]{0:T(128)} %get-tuple-element.54) | copy-start | bytes 772
  149.4 13.1 %copy-start.56 = (f32[64]{0:T(128)S(1)}, f32[64]{0:T(128)}, u32[]{:S(2)}) copy-start(f32[64]{0:T(128)} %get-tuple-element.53) | copy-start | bytes 772
  150.3 13.1 %copy-start.46 = (f32[64]{0:T(128)S(1)}, f32[64]{0:T(128)}, u32[]{:S(2)}) copy-start(f32[64]{0:T(128)} %get-tuple-element.52) | copy-start | bytes 772
  151.1 13.1 %copy-start.38 = (f32[64]{0:T(128)S(1)}, f32[64]{0:T(128)}, u32[]{:S(2)}) copy-start(f32[64]{0:T(128)} %get-tuple-element.47) | copy-start | bytes 772
  151.1 13.1 %copy-start.90 = (f32[64]{0:T(128)S(1)}, f32[64]{0:T(128)}, u32[]{:S(2)}) copy-start(f32[64]{0:T(128)} %get-tuple-element.230) | copy-start | bytes 772
  151.9 13.1 %copy-start.32 = (f32[64]{0:T(128)S(1)}, f32[64]{0:T(128)}, u32[]{:S(2)}) copy-start(f32[64]{0:T(128)} %get-tuple-element.51) | copy-start | bytes 772
  151.9 13.1 %copy-start.80 = (f32[64]{0:T(128)S(1)}, f32[64]{0:T(128)}, u32[]{:S(2)}) copy-start(f32[64]{0:T(128)} %get-tuple-element.237) | copy-start | bytes 772
  152.6 13.1 %copy-start.28 = (f32[64]{0:T(128)S(1)}, f32[64]{0:T(128)}, u32[]{:S(2)}) copy-start(f32[64]{0:T(128)} %get-tuple-element.50) | copy-start | bytes 772
  152.6 13.1 %copy-start.70 = (f32[64]{0:T(128)S(1)}, f32[64]{0:T(128)}, u32[]{:S(2)}) copy-start(f32[64]{0:T(128)} %get-tuple-element.236) | copy-start | bytes 772
  154.3 13.0 %copy-start.24 = (f32[64]{0:T(128)S(1)}, f32[64]{0:T(128)}, u32[]{:S(2)}) copy-start(f32[64]{0:T(128)} %copy-done.23) | copy-start | bytes 772
  156.8 13.1 %copy-start.30 = (f32[64]{0:T(128)S(1)}, f32[64]{0:T(128)}, u32[]{:S(2)}) copy-start(f32[64]{0:T(128)} %get-tuple-element.231) | copy-start | bytes 772
  156.8 13.1 %copy-start.74 = (f32[64]{0:T(128)S(1)}, f32[64]{0:T(128)}, u32[]{:S(2)}) copy-start(f32[64]{0:T(128)} %get-tuple-element.182) | copy-start | bytes 772
  156.8 13.1 %copy-start.128 = (f32[64]{0:T(128)S(1)}, f32[64]{0:T(128)}, u32[]{:S(2)}) copy-start(f32[64]{0:T(128)} %get-tuple-element.134) | copy-start | bytes 772
  157.7 13.1 %copy-start.22 = (f32[64]{0:T(128)S(1)}, f32[64]{0:T(128)}, u32[]{:S(2)}) copy-start(f32[64]{0:T(128)} %get-tuple-element.229) | copy-start | bytes 772
  157.7 13.1 %copy-start.64 = (f32[64]{0:T(128)S(1)}, f32[64]{0:T(128)}, u32[]{:S(2)}) copy-start(f32[64]{0:T(128)} %get-tuple-element.181) | copy-start | bytes 772
  157.7 13.1 %copy-start.118 = (f32[64]{0:T(128)S(1)}, f32[64]{0:T(128)}, u32[]{:S(2)}) copy-start(f32[64]{0:T(128)} %get-tuple-element.133) | copy-start | bytes 772
  158.5 13.2 %copy-start.20 = (f32[64]{0:T(128)S(1)}, f32[64]{0:T(128)}, u32[]{:S(2)}) copy-start(f32[64]{0:T(128)} %get-tuple-element.228) | copy-start | bytes 772
  158.5 13.2 %copy-start.54 = (f32[64]{0:T(128)S(1)}, f32[64]{0:T(128)}, u32[]{:S(2)}) copy-start(f32[64]{0:T(128)} %get-tuple-element.180) | copy-start | bytes 772
  158.5 13.2 %copy-start.107 = (f32[64]{0:T(128)S(1)}, f32[64]{0:T(128)}, u32[]{:S(2)}) copy-start(f32[64]{0:T(128)} %get-tuple-element.132) | copy-start | bytes 772
  (255 other events, 1484.7 us)
where the time goes:
time: 240 us; the launch traced here: 238 us
  local copies, waits for them, and re-layouts  85.1 us (35%)
  other arithmetic  73.1 us (30%)
  starting transfers between devices  30.3 us (13%)
  blocking collectives  27.3 us (11%)
  matrix products  8.93 us (4%)
  waiting for transfers between devices  7.63 us (3%)
  between operations  5.7 us (2%)
    unnamed x70, other arithmetic  48.4 us
    unnamed x583, local copies, waits for them, and re-layouts  33.3 us
    all_to_all x1, blocking collectives, body(): lax.all_to_all(projected.reshape(owners, span_chan, coeffs, atom_count),...  27.3 us
    all_to_all x1, starting transfers between devices, body(): lax.all_to_all(outgoing, 'graph', split_axis=2, concat_axis=2, tiled=True)  15.5 us
    slice x8, local copies, waits for them, and re-layouts, body(): weight = weight_full[degree].astype(jnp.bfloat16)  10.9 us
    mul x13, local copies, waits for them, and re-layouts, rotate(): wig_rows[first_row + position * span_cols + column][None, :]  8.54 us
    convert_element_type x2, local copies, waits for them, and re-layouts, body(): source = source.astype(jnp.float32)  8.33 us
    gather x1, local copies, waits for them, and re-layouts, body(): lookup[:, :, edge_source]  7.66 us
  transfers between devices with their start and end apart: 3, of which 1 were waited for; matrix products, arithmetic and copies ran while one was open for 20% of the time, Pallas kernels for 0%

commit v1 on v0

--- a/solution.py
+++ b/solution.py
@@ -190,7 +190,12 @@
     per_owner = edge_source.shape[0] // owners
     first_edge = quarter * per_owner
     outgoing = node_feats[:, :, send_list]
-    arrived = lax.all_to_all(outgoing, "graph", split_axis=2, concat_axis=2, tiled=True)
+    arrived = jnp.concatenate(
+        lax.all_to_all(
+            jnp.stack(jnp.split(outgoing, lax.axis_size("graph"), axis=2)), "graph", 0, 0
+        ),
+        axis=2,
+    )
     packed = jnp.concatenate(
         [norm_gain, project_weight.astype(jnp.float32).reshape(levels, -1)], axis=1
     )

time: 240 us -> 239 us (level)
  other arithmetic: 73.1 us -> 69.4 us
    convert_element_type x0 -> x1, other arithmetic: none -> 3.9 us  [body(): source = source.astype(jnp.float32)]
    unnamed x70, other arithmetic: 48.4 us -> 44.7 us
    unnamed x583 -> x619, local copies, waits for them, and re-layouts: 33.3 us -> 33.9 us
  transfers between devices with their start and end apart: 3 -> 3, of which waited for: 1 -> 1; matrix products, arithmetic and copies ran while one was open for 20% -> 21% of each run, Pallas kernels for 0% -> 0%
where the time goes in v1:
time: 239 us; the launch traced here: 237 us
  local copies, waits for them, and re-layouts  86.6 us (36%)
  other arithmetic  69.4 us (29%)
  starting transfers between devices  30.3 us (13%)
  blocking collectives  27.1 us (11%)
  matrix products  10.2 us (4%)
  waiting for transfers between devices  7.06 us (3%)
  between operations  5.95 us (2%)
    unnamed x70, other arithmetic  44.7 us
    unnamed x619, local copies, waits for them, and re-layouts  33.9 us
    all_to_all x1, blocking collectives, body(): lax.all_to_all(projected.reshape(owners, span_chan, coeffs, atom_count),...  27.1 us
    all_to_all x1, starting transfers between devices, body(): lax.all_to_all(jnp.stack(jnp.split(outgoing, lax.axis_size('graph'), axis...  15.5 us
    slice x8, local copies, waits for them, and re-layouts, body(): weight = weight_full[degree].astype(jnp.bfloat16)  11.7 us
    mul x13, local copies, waits for them, and re-layouts, rotate(): wig_rows[first_row + position * span_cols + column][None, :]  8.58 us
    convert_element_type x2, local copies, waits for them, and re-layouts, body(): source = source.astype(jnp.float32)  8.37 us
    gather x1, local copies, waits for them, and re-layouts, body(): lookup[:, :, edge_source]  7.55 us
  transfers between devices with their start and end apart: 3, of which 1 were waited for; matrix products, arithmetic and copies ran while one was open for 21% of the time, Pallas kernels for 0%

profile of v1, /device:TPU:2, one launch (start us, length us, event | category | flops | bytes accessed | tf_op | source)
XLA Modules:
  0.0 236.7 jit_solution(15608196894159535433)
XLA Ops:
  3.8 2.0 reshape.3043
  5.8 15.5 %all-to-all-start.1 = ((bf16[32,2,1568]{2,1,0:T(2,128)(2,1)}), bf16[32,2,1568]{2,1,0:T(2,128)(2,1)S(1)}, u32[]{:S(2)}, u32[]{:S(2)}) async-start(bf16[32,2,1568]{2,1,0:T(2,128)(2,1)} %reshape.3043), calls=%async_computation.1 | async-start | bytes 425984 | tf_op jit(solution)/shard_map/all_to_all | solution.py:194
  30.2 1.2 compare_select_fusion.2
  35.0 7.1 %all-to-all-done.1 = bf16[32,2,1568]{2,1,0:T(2,128)(2,1)S(1)} async-done(((bf16[32,2,1568]{2,1,0:T(2,128)(2,1)}), bf16[32,2,1568]{2,1,0:T(2,128)(2,1)S(1)}, u32[]{:S(2)}, u32[]{:S(2)}) %all-to-all-start.1) | async-done | bytes 200736 | tf_op jit(solution)/shard_map/all_to_all | solution.py:194
  42.9 7.5 %all-to-all-start = ((f32[16,7,1032]{2,1,0:T(8,128)}), f32[16,7,1032]{2,1,0:T(8,128)S(1)}, u32[]{:S(2)}, u32[]{:S(2)}) async-start(f32[16,7,1032]{2,1,0:T(8,128)} %broadcast_in_dim.56), calls=%async_computation | async-start | bytes 1179648 | tf_op jit(solution)/shard_map/all_to_all | solution.py:202
  50.4 2.5 %reshape.3044 = bf16[32,8,8,49]{3,2,1,0:T(8,128)(2,1)S(1)} reshape(bf16[32,2,1568]{2,1,0:T(2,128)(2,1)} %copy-done.10) | data formatting | bytes 401408
  53.0 7.5 %gather_fusion.1 = bf16[1024,49,8]{1,2,0:T(8,128)(2,1)} fusion(bf16[49,8,320]{0,1,2:T(8,128)(2,1)S(1)} %pad_maximum_fusion, s32[1024]{0:T(1024)S(1)} %get-tuple-element.263), kind=kCustom, calls=%fused_computation.1 | custom fusion | bytes 1609728 | tf_op jit(solution)/shard_map/gather | solution.py:213
  60.6 3.1 %bitcast_bitcast_fusion = bf16[1024,8,49]{2,1,0:T(8,128)(2,1)} fusion(bf16[1024,49,8]{1,2,0:T(8,128)(2,1)} %gather_fusion.1), kind=kLoop, calls=%fused_computation.555 | loop fusion | bytes 1605632
  63.7 5.8 %reshape.3045 = bf16[16,2,12544]{2,1,0:T(2,128)(2,1)} reshape(bf16[1024,8,49]{2,1,0:T(8,128)(2,1)} %bitcast_bitcast_fusion) | data formatting | bytes 1605632
  69.5 7.4 %all-to-all-start.2 = ((bf16[16,2,12544]{2,1,0:T(2,128)(2,1)}), bf16[16,2,12544]{2,1,0:T(2,128)(2,1)}, u32[]{:S(2)}, u32[]{:S(2)}) async-start(bf16[16,2,12544]{2,1,0:T(2,128)(2,1)} %reshape.3045), calls=%async_computation.2 | async-start | bytes 1605632 | tf_op jit(solution)/shard_map/all_to_all | solution.py:212
  79.6 1.8 copy.231
  81.5 1.3 fusion.73
  82.7 1.8 copy.276
  84.6 1.7 copy.272
  86.3 1.8 copy.268
  88.1 1.8 copy.264
  89.8 1.7 copy.260
  93.7 7.8 %reshape.3046 = bf16[1024,8,49]{2,1,0:T(8,128)(2,1)} reshape(bf16[16,2,12544]{2,1,0:T(2,128)(2,1)} %all-to-all-done.2) | data formatting | bytes 1605632
  101.5 3.1 %multiply_reduce_fusion = f32[49,1024]{0,1:T(8,128)S(1)} fusion(bf16[1024,8,49]{2,1,0:T(8,128)(2,1)} %reshape.3046), kind=kLoop, calls=%fused_computation.6 | loop fusion | flops 1154048 | bytes 1003520 | tf_op jit(solution)/shard_map/reduce_sum | solution.py:216
  105.7 3.9 %bitcast_convert_fusion.3 = f32[49,8,1024]{0,1,2:T(8,128)} fusion(bf16[1024,8,49]{2,1,0:T(8,128)(2,1)} %reshape.3046), kind=kLoop, calls=%fused_computation.554 | loop fusion | flops 401408 | bytes 2408448 | tf_op jit(solution)/shard_map/convert_element_type | solution.py:215
  110.4 5.6 %copy.238 = f32[49,16,8,64]{3,2,1,0:T(8,128)} copy(f32[49,16,8,64]{0,2,3,1:T(8,128)} %bitcast.875) | data formatting | bytes 3211264 | tf_op jit(solution)/shard_map/convert_element_type | solution.py:215
  116.0 2.8 %copy.240 = f32[49,128,64]{1,2,0:T(8,128)S(1)} copy(f32[49,128,64]{2,1,0:T(8,128)} %bitcast.876) | data formatting | bytes 3211264 | tf_op jit(solution)/shard_map/convert_element_type | solution.py:215
  120.6 1.4 constant_dynamic-update-slice_fusion.61
  122.0 1.6 constant_dynamic-update-slice_fusion.57
  133.1 1.4 constant_dynamic-update-slice_fusion.50
  141.4 1.4 fusion.9
  194.3 1.9 copy.337
  196.2 3.5 %reshape.3047 = f32[16,1,25088]{2,1,0:T(1,128)S(1)} reshape(f32[16,49,8,64]{3,2,1,0:T(8,128)} %bitcast.877) | data formatting | bytes 3211264
  199.8 27.1 %all_to_all.24 = f32[16,1,25088]{2,1,0:T(1,128)S(1)} all-to-all(f32[16,1,25088]{2,1,0:T(1,128)S(1)} %reshape.3047), channel_id=1, replica_groups=mesh['graph'=32,'irreps'=16] {'irreps'}, dimensions={0} | all-to-all | bytes 3211264 | tf_op jit(solution)/shard_map/all_to_all | solution.py:252
  227.4 4.5 %reduce.4 = f32[16,25088]{1,0:T(8,128)S(1)} reduce(f32[16,1,25088]{2,1,0:T(1,128)S(1)} %all_to_all.24, f32[]{:T(128)} %broadcast.1939), dimensions={1}, to_apply=%all_to_all.19.reduce_sub_computation | reduce | bytes 3211268 | tf_op jit(solution)/shard_map/all_to_all | solution.py:252
  231.9 2.0 reshape.3048
  233.9 2.2 bitcast_reduce_fusion
  (796 shorter events, 89.2 us)
Async XLA Ops:
  0.0 141.4 %copy-start = (bf16[896,896]{1,0:T(8,128)(2,1)S(1)}, bf16[896,896]{1,0:T(8,128)(2,1)}, u32[]{:S(2)}) copy-start(bf16[896,896]{1,0:T(8,128)(2,1)} %param.32) | copy-start | bytes 4816900
  0.0 31.4 %copy-start.20 = (bf16[7,128,8]{1,2,0:T(8,128)(2,1)S(1)}, bf16[7,128,8]{1,2,0:T(8,128)(2,1)}, u32[]{:S(2)}) copy-start(bf16[7,128,8]{1,2,0:T(8,128)(2,1)} %param.35) | copy-start | bytes 43012
  3.5 29.7 %copy-start.276 = (s32[1024]{0:T(1024)S(1)}, s32[1024]{0:T(1024)}, u32[]{:S(2)}) copy-start(s32[1024]{0:T(1024)} %param.24) | copy-start | bytes 12292
  3.5 30.4 %copy-start.277 = (f32[7,8]{1,0:T(8,128)S(1)}, f32[7,8]{1,0:T(8,128)}, u32[]{:S(2)}) copy-start(f32[7,8]{1,0:T(8,128)} %param.21) | copy-start | bytes 676
  3.6 30.4 %copy-start.280 = (bf16[512,128]{1,0:T(8,128)(2,1)S(1)}, bf16[512,128]{1,0:T(8,128)(2,1)}, u32[]{:S(2)}) copy-start(bf16[512,128]{1,0:T(8,128)(2,1)} %param.29) | copy-start | bytes 393220
  5.8 36.2 %all-to-all-start.1 = ((bf16[32,2,1568]{2,1,0:T(2,128)(2,1)}), bf16[32,2,1568]{2,1,0:T(2,128)(2,1)S(1)}, u32[]{:S(2)}, u32[]{:S(2)}) async-start(bf16[32,2,1568]{2,1,0:T(2,128)(2,1)} %reshape.3043), calls=%async_computation.1 | async-start | bytes 425984 | tf_op jit(solution)/shard_map/all_to_all | solution.py:194
  42.9 26.6 %all-to-all-start = ((f32[16,7,1032]{2,1,0:T(8,128)}), f32[16,7,1032]{2,1,0:T(8,128)S(1)}, u32[]{:S(2)}, u32[]{:S(2)}) async-start(f32[16,7,1032]{2,1,0:T(8,128)} %broadcast_in_dim.56), calls=%async_computation | async-start | bytes 1179648 | tf_op jit(solution)/shard_map/all_to_all | solution.py:202
  63.7 13.8 %copy-start.2 = (s32[64]{0:T(128)S(1)}, s32[64]{0:T(128)}, u32[]{:S(2)}) copy-start(s32[64]{0:T(128)} %param.22) | copy-start | bytes 772
  69.5 24.2 %all-to-all-start.2 = ((bf16[16,2,12544]{2,1,0:T(2,128)(2,1)}), bf16[16,2,12544]{2,1,0:T(2,128)(2,1)}, u32[]{:S(2)}, u32[]{:S(2)}) async-start(bf16[16,2,12544]{2,1,0:T(2,128)(2,1)} %reshape.3045), calls=%async_computation.2 | async-start | bytes 1605632 | tf_op jit(solution)/shard_map/all_to_all | solution.py:212
  143.8 13.3 %copy-start.55 = (f32[64]{0:T(128)S(1)}, f32[64]{0:T(128)}, u32[]{:S(2)}) copy-start(f32[64]{0:T(128)} %get-tuple-element.57) | copy-start | bytes 772
  144.7 13.2 %copy-start.51 = (f32[64]{0:T(128)S(1)}, f32[64]{0:T(128)}, u32[]{:S(2)}) copy-start(f32[64]{0:T(128)} %get-tuple-element.56) | copy-start | bytes 772
  145.6 13.2 %copy-start.47 = (f32[64]{0:T(128)S(1)}, f32[64]{0:T(128)}, u32[]{:S(2)}) copy-start(f32[64]{0:T(128)} %get-tuple-element.55) | copy-start | bytes 772
  146.4 13.1 %copy-start.43 = (f32[64]{0:T(128)S(1)}, f32[64]{0:T(128)}, u32[]{:S(2)}) copy-start(f32[64]{0:T(128)} %get-tuple-element.54) | copy-start | bytes 772
  147.2 13.1 %copy-start.39 = (f32[64]{0:T(128)S(1)}, f32[64]{0:T(128)}, u32[]{:S(2)}) copy-start(f32[64]{0:T(128)} %get-tuple-element.53) | copy-start | bytes 772
  147.2 13.1 %copy-start.97 = (f32[64]{0:T(128)S(1)}, f32[64]{0:T(128)}, u32[]{:S(2)}) copy-start(f32[64]{0:T(128)} %get-tuple-element.98) | copy-start | bytes 772
  148.0 13.2 %copy-start.35 = (f32[64]{0:T(128)S(1)}, f32[64]{0:T(128)}, u32[]{:S(2)}) copy-start(f32[64]{0:T(128)} %get-tuple-element.52) | copy-start | bytes 772
  148.0 13.2 %copy-start.89 = (f32[64]{0:T(128)S(1)}, f32[64]{0:T(128)}, u32[]{:S(2)}) copy-start(f32[64]{0:T(128)} %get-tuple-element.97) | copy-start | bytes 772
  148.8 13.2 %copy-start.33 = (f32[64]{0:T(128)S(1)}, f32[64]{0:T(128)}, u32[]{:S(2)}) copy-start(f32[64]{0:T(128)} %get-tuple-element.47) | copy-start | bytes 772
  148.8 13.2 %copy-start.83 = (f32[64]{0:T(128)S(1)}, f32[64]{0:T(128)}, u32[]{:S(2)}) copy-start(f32[64]{0:T(128)} %get-tuple-element.96) | copy-start | bytes 772
  149.6 13.2 %copy-start.31 = (f32[64]{0:T(128)S(1)}, f32[64]{0:T(128)}, u32[]{:S(2)}) copy-start(f32[64]{0:T(128)} %get-tuple-element.51) | copy-start | bytes 772
  149.6 13.2 %copy-start.77 = (f32[64]{0:T(128)S(1)}, f32[64]{0:T(128)}, u32[]{:S(2)}) copy-start(f32[64]{0:T(128)} %get-tuple-element.95) | copy-start | bytes 772
  150.4 13.1 %copy-start.29 = (f32[64]{0:T(128)S(1)}, f32[64]{0:T(128)}, u32[]{:S(2)}) copy-start(f32[64]{0:T(128)} %get-tuple-element.50) | copy-start | bytes 772
  150.5 13.1 %copy-start.71 = (f32[64]{0:T(128)S(1)}, f32[64]{0:T(128)}, u32[]{:S(2)}) copy-start(f32[64]{0:T(128)} %get-tuple-element.94) | copy-start | bytes 772
  152.1 13.1 %copy-start.61 = (f32[64]{0:T(128)S(1)}, f32[64]{0:T(128)}, u32[]{:S(2)}) copy-start(f32[64]{0:T(128)} %get-tuple-element.92) | copy-start | bytes 772
  152.9 13.2 %copy-start.27 = (f32[64]{0:T(128)S(1)}, f32[64]{0:T(128)}, u32[]{:S(2)}) copy-start(f32[64]{0:T(128)} %get-tuple-element.46) | copy-start | bytes 772
  152.9 13.2 %copy-start.57 = (f32[64]{0:T(128)S(1)}, f32[64]{0:T(128)}, u32[]{:S(2)}) copy-start(f32[64]{0:T(128)} %get-tuple-element.91) | copy-start | bytes 772
  152.9 13.2 %copy-start.99 = (f32[64]{0:T(128)S(1)}, f32[64]{0:T(128)}, u32[]{:S(2)}) copy-start(f32[64]{0:T(128)} %get-tuple-element.137) | copy-start | bytes 772
  153.7 13.1 %copy-start.23 = (f32[64]{0:T(128)S(1)}, f32[64]{0:T(128)}, u32[]{:S(2)}) copy-start(f32[64]{0:T(128)} %get-tuple-element.45) | copy-start | bytes 772
  153.7 13.1 %copy-start.53 = (f32[64]{0:T(128)S(1)}, f32[64]{0:T(128)}, u32[]{:S(2)}) copy-start(f32[64]{0:T(128)} %get-tuple-element.90) | copy-start | bytes 772
  153.8 13.1 %copy-start.91 = (f32[64]{0:T(128)S(1)}, f32[64]{0:T(128)}, u32[]{:S(2)}) copy-start(f32[64]{0:T(128)} %get-tuple-element.136) | copy-start | bytes 772
  154.6 13.1 %copy-start.49 = (f32[64]{0:T(128)S(1)}, f32[64]{0:T(128)}, u32[]{:S(2)}) copy-start(f32[64]{0:T(128)} %get-tuple-element.89) | copy-start | bytes 772
  154.6 13.1 %copy-start.85 = (f32[64]{0:T(128)S(1)}, f32[64]{0:T(128)}, u32[]{:S(2)}) copy-start(f32[64]{0:T(128)} %get-tuple-element.134) | copy-start | bytes 772
  (259 other events, 1400.3 us)
